TPU v7x, 256 devices: a whole 4x4x8 slice. The times are simulated.
256 devices in a mesh: dom: 64 (over z, x, core), sub: 4 (over y).
Axes of the slice: x: 4, y: 4, z: 8, core: 2. Of those that a mesh axis runs over, the one named last changes fastest.
Arguments:
- excitation: bfloat16 [64, 1536, 64], P('dom', 'sub'), may hold values from -6 to 6
- local_inverse: bfloat16 [64, 1536, 1536], P('dom', 'sub'), as said below
- aggregation: bfloat16 [64, 1024, 1536], P('dom', None, 'sub'), may hold values from -0.15625 to 0.15625
- disaggregation: bfloat16 [64, 1536, 1024], P('dom', 'sub'), may hold values from -0.1875 to 0.1875
- translation: float32 [64, 6, 2, 512], P('dom'), may hold values from -1.5 to 1.5
- partners: int32 [64, 6], P('dom'), may hold values from 0 to 63, as said below
- list_counts: int32 [64], P('dom'), may hold values from 2 to 6
- sweep_order: int32 [64], replicated, may hold values from 0 to 63, as said below
Outputs:
- currents: float32 [64, 1536, 64], P('dom', 'sub')
Inputs may be any that keep to these rules, and one draw needn't show every extreme that they name: `partners`: row d names 6 different subdomains, none equal to d; only its first list_counts[d] slots are used. `local_inverse`: each subdomain's matrix is the identity plus independent entries of spread 0.6 / sqrt(1536). `sweep_order`: every subdomain has a position of its own.
All inputs are finite; a program needn't handle non-finite values.
Results may differ from a plain program's by a relative error of at most 0.03.
Values may be sent and summed in bfloat16 or wider, within the bound.
No kernel may reach another device: no remote copies, remote signals or barrier semaphores. Data moves between devices by JAX's collectives and lax.ppermute only.
A program may use at most 64 MiB of HBM per device.

v0:
```python
import jax
import jax.numpy as jnp
from jax import lax
from jax.sharding import PartitionSpec as P

SEGMENTS = 8
CONTRACT_FIRST = (((0,), (1,)), ((), ()))
CONTRACT_LAST = (((1,), (1,)), ((), ()))


def rotate(real_weight, imag_weight, pattern):
    samples = real_weight.shape[-1]
    values = pattern.astype(jnp.float32)
    real_part = values[..., :samples]
    imag_part = values[..., samples:]
    return jnp.concatenate(
        [
            real_weight * real_part - imag_weight * imag_part,
            real_weight * imag_part + imag_weight * real_part,
        ],
        axis=-1,
    )


def local(
    excitation,
    local_inverse,
    aggregation,
    disaggregation,
    translation,
    partners,
    list_counts,
    sweep_order,
):
    excite_rows = excitation[0]
    inverse_rows = local_inverse[0]
    agg_columns = aggregation[0]
    disagg_rows = disaggregation[0]
    trans_rows = translation[0]
    partner_row = partners[0]

    def apply_inverse(shard_rows):
        return jnp.dot(inverse_rows, shard_rows, preferred_element_type=jnp.float32)

    solved = apply_inverse(lax.all_gather(excite_rows, "sub", axis=0, tiled=True))
    solved_half = solved.astype(jnp.bfloat16)
    incident = lax.psum_scatter(
        lax.dot_general(
            solved_half, agg_columns, CONTRACT_FIRST, preferred_element_type=jnp.float32
        ).astype(jnp.bfloat16),
        "sub",
        scatter_dimension=0,
        tiled=True,
    ).astype(jnp.float32)
    spread = apply_inverse(lax.all_gather(disagg_rows, "sub", axis=0, tiled=True))
    spread_half = spread.astype(jnp.bfloat16)
    partial_map = lax.dot_general(
        spread_half, agg_columns, CONTRACT_FIRST, preferred_element_type=jnp.float32
    )
    coupling = lax.psum(partial_map.astype(jnp.bfloat16), "sub")
    domains = sweep_order.shape[0]
    segment_of = sweep_order * SEGMENTS // domains
    own_index = lax.axis_index("dom")
    my_segment = segment_of[own_index]
    slot_live = jnp.arange(partner_row.shape[0], dtype=jnp.int32) < list_counts[0]
    domain_ids = jnp.arange(domains, dtype=jnp.int32)
    incoming = jnp.zeros(incident.shape, jnp.float32)
    for segment_k in range(SEGMENTS - 1):
        pattern = (
            incident
            - jnp.dot(incoming.astype(jnp.bfloat16), coupling, preferred_element_type=jnp.float32)
        ).astype(jnp.bfloat16)
        pattern = jnp.where(my_segment == segment_k, pattern, jnp.zeros_like(pattern))
        make_piece = lax.all_gather(pattern[None], "dom", axis=0, tiled=True)
        count = make_piece.shape[0]
        make_senders = jnp.arange(count, dtype=jnp.int32)
        sender_segment = jnp.sum(
            jnp.where(domain_ids[None, :] == make_senders[:, None], segment_of[None, :], 0), axis=1
        )
        sender_live = sender_segment == segment_k
        match = (
            (partner_row[:, None] == make_senders[None, :])
            & slot_live[:, None]
            & sender_live[None, :]
            & (segment_k < my_segment)
        )
        weights = jnp.sum(
            jnp.where(match[:, :, None, None], trans_rows[:, None, :, :], 0.0), axis=0
        )
        terms = rotate(weights[:, 0][:, None, :], weights[:, 1][:, None, :], make_piece)
        incoming = incoming + jnp.sum(terms, axis=0)
    fields = lax.all_gather(incoming.astype(jnp.bfloat16), "sub", axis=0, tiled=True)
    currents = solved - lax.dot_general(
        spread_half, fields, CONTRACT_LAST, preferred_element_type=jnp.float32
    )
    return currents[None]


def solution(mesh):
    in_specs = (
        P("dom", "sub", None),
        P("dom", "sub", None),
        P("dom", None, "sub"),
        P("dom", "sub", None),
        P("dom", None, None, None),
        P("dom", None),
        P("dom"),
        P(),
    )
    out_specs = P("dom", "sub", None)
    return jax.shard_map(local, mesh=mesh, in_specs=in_specs, out_specs=out_specs, check_vma=False)
```

profile of v0, /device:TPU:8, one launch (start us, length us, event | category | flops | bytes accessed | tf_op | source)
XLA Modules:
  0.0 727.2 jit_solution(1331858626277878469)
XLA Ops:
  6.5 0.7 all-gather.18.cloned.1.call-update
  7.3 12.7 %all-gather = bf16[1,1536,64]{1,2,0:T(8,128)(2,1)S(1)} all-gather(bf16[1,384,64]{1,2,0:T(8,128)(2,1)} %param.8), channel_id=2, replica_groups=mesh['dom'=64,'sub'=4] {'sub'}, dimensions={1}, use_global_device_ids=true | all-gather | bytes 245760 | tf_op jit(solution)/shard_map/all_gather | solution.py:45
  20.0 0.5 fusion.6
  20.5 0.6 copy-done.4
  21.1 1.0 convolution_convert_fusion.1
  22.2 0.0 all-reduce.2.cloned.1.call-start
  22.2 31.2 %all-gather.18.cloned.1.call-done = bf16[1,1536,1024]{2,1,0:T(8,128)(2,1)} async-done(((bf16[1,384,1024]{2,1,0:T(8,128)(2,1)}), bf16[1,1536,1024]{2,1,0:T(8,128)(2,1)}) %all-gather.18.cloned.1.call-update) | async-done | bytes 3145744 | tf_op jit(solution)/shard_map/all_gather | solution.py:55
  53.4 3.3 fusion.2
  56.7 0.9 copy-done.6
  57.6 2.6 convolution_convert_fusion
  60.2 0.0 all-gather.20.cloned.1.call-start
  60.3 0.7 dynamic_slice.3
  61.7 16.3 %reduce-scatter.2.cloned.1.call-done = bf16[16,1024]{1,0:T(8,128)(2,1)} async-done(((bf16[64,1024]{1,0:T(8,128)(2,1)}), bf16[16,1024]{1,0:T(8,128)(2,1)}) %reduce-scatter.2.cloned.1.call-update) | async-done | bytes 32784 | tf_op jit(solution)/shard_map/reduce_scatter | solution.py:47
  78.0 66.8 %all-reduce.2.cloned.1.call-done = bf16[1024,1024]{1,0:T(8,128)(2,1)} async-done(((bf16[1024,1024]{1,0:T(8,128)(2,1)}), bf16[1024,1024]{1,0:T(8,128)(2,1)}) %all-reduce.2.cloned.1.call-update) | async-done | bytes 2097168 | tf_op jit(solution)/shard_map/psum | solution.py:60
  144.8 2.6 fusion.10
  147.4 0.0 all-gather.22.cloned.1.call-start
  153.7 0.1 select_reduce_fusion.7
  153.8 0.1 fusion.42
  153.9 1.9 select_reduce_fusion
  155.8 70.0 %all-gather.20.cloned.1.call-done = bf16[1024,1024]{1,0:T(8,128)(2,1)} async-done(((bf16[16,1024]{1,0:T(8,128)(2,1)}), bf16[1024,1024]{1,0:T(8,128)(2,1)}) %all-gather.20.cloned.1.call-update) | async-done | bytes 2097168 | tf_op jit(solution)/shard_map/all_gather | solution.py:74
  225.8 2.1 convert
  227.8 0.8 multiply_subtract_fusion.6
  228.7 0.2 maximum_reduce_fusion
  228.9 1.3 copy-done.2
  230.2 1.0 fusion.22
  232.0 1.7 slice_bitcast_fusion.11
  233.7 72.6 %all-gather.22.cloned.1.call-done = bf16[1024,1024]{1,0:T(8,128)(2,1)} async-done(((bf16[16,1024]{1,0:T(8,128)(2,1)}), bf16[1024,1024]{1,0:T(8,128)(2,1)}) %all-gather.22.cloned.1.call-update) | async-done | bytes 2097168 | tf_op jit(solution)/shard_map/all_gather | solution.py:74
  306.3 2.1 convert.1
  308.5 0.8 multiply_subtract_fusion.5
  309.3 0.2 maximum_reduce_fusion.1
  309.6 0.6 copy-done.9
  310.2 1.0 fusion.21
  311.9 0.7 slice_bitcast_fusion.9
  312.6 73.6 %all-gather.24.cloned.1.call-done = bf16[1024,1024]{1,0:T(8,128)(2,1)} async-done(((bf16[16,1024]{1,0:T(8,128)(2,1)}), bf16[1024,1024]{1,0:T(8,128)(2,1)}) %all-gather.24.cloned.1.call-update) | async-done | bytes 2097168 | tf_op jit(solution)/shard_map/all_gather | solution.py:74
  386.3 2.1 convert.2
  388.4 0.8 multiply_subtract_fusion.4
  389.2 0.2 maximum_reduce_fusion.2
  389.5 0.6 copy-done.10
  390.1 1.0 fusion.20
  391.1 0.0 all-gather.28.cloned.1.call-start
  391.8 0.7 slice_bitcast_fusion.7
  392.5 73.7 %all-gather.26.cloned.1.call-done = bf16[1024,1024]{1,0:T(8,128)(2,1)} async-done(((bf16[16,1024]{1,0:T(8,128)(2,1)}), bf16[1024,1024]{1,0:T(8,128)(2,1)}) %all-gather.26.cloned.1.call-update) | async-done | bytes 2097168 | tf_op jit(solution)/shard_map/all_gather | solution.py:74
  466.2 2.1 convert.3
  468.3 0.8 multiply_subtract_fusion.3
  469.1 0.2 maximum_reduce_fusion.3
  469.3 1.0 fusion.19
  470.4 0.2 all-gather.30.cloned.1.call-start
  471.3 74.1 %all-gather.28.cloned.1.call-done = bf16[1024,1024]{1,0:T(8,128)(2,1)} async-done(((bf16[16,1024]{1,0:T(8,128)(2,1)}), bf16[1024,1024]{1,0:T(8,128)(2,1)}) %all-gather.28.cloned.1.call-update) | async-done | bytes 2097168 | tf_op jit(solution)/shard_map/all_gather | solution.py:74
  545.4 2.1 convert.4
  547.5 0.8 multiply_subtract_fusion.2
  548.3 0.2 maximum_reduce_fusion.4
  548.6 1.0 fusion.18
  549.6 0.0 all-gather.32.cloned.1.call-start
  550.4 74.3 %all-gather.30.cloned.1.call-done = bf16[1024,1024]{1,0:T(8,128)(2,1)} async-done(((bf16[16,1024]{1,0:T(8,128)(2,1)}), bf16[1024,1024]{1,0:T(8,128)(2,1)}) %all-gather.30.cloned.1.call-update) | async-done | bytes 2097168 | tf_op jit(solution)/shard_map/all_gather | solution.py:74
  624.7 2.1 convert.5
  626.7 0.8 multiply_subtract_fusion.1
  627.5 0.2 maximum_reduce_fusion.5
  627.8 1.0 fusion.17
  628.8 75.0 %all-gather.32.cloned.1.call-done = bf16[1024,1024]{1,0:T(8,128)(2,1)} async-done(((bf16[16,1024]{1,0:T(8,128)(2,1)}), bf16[1024,1024]{1,0:T(8,128)(2,1)}) %all-gather.32.cloned.1.call-update) | async-done | bytes 2097168 | tf_op jit(solution)/shard_map/all_gather | solution.py:74
  703.9 2.1 convert.6
  706.0 0.8 multiply_subtract_fusion
  706.8 0.2 maximum_reduce_fusion.6
  707.0 12.3 %all_gather.39 = bf16[64,1024]{1,0:T(8,128)(2,1)S(1)} all-gather(bf16[16,1024]{1,0:T(8,128)(2,1)S(1)} %add_convert_fusion), channel_id=1, replica_groups=mesh['dom'=64,'sub'=4] {'sub'}, dimensions={0}, use_global_device_ids=true | all-gather | bytes 163840 | tf_op jit(solution)/shard_map/all_gather | solution.py:92
  719.4 1.0 fusion.8
  (59 shorter events, 0.5 us)
Async XLA Ops:
  6.5 13.4 %copy-start = (bf16[1,384,1536]{2,1,0:T(8,128)(2,1)S(1)}, bf16[1,384,1536]{2,1,0:T(8,128)(2,1)}, u32[]{:S(2)}) copy-start(bf16[1,384,1536]{2,1,0:T(8,128)(2,1)} %param.9) | copy-start | bytes 3538948
  6.5 14.6 %copy-start.8 = (bf16[1,1024,384]{2,1,0:T(8,128)(2,1)S(1)}, bf16[1,1024,384]{2,1,0:T(8,128)(2,1)}, u32[]{:S(2)}) copy-start(bf16[1,1024,384]{2,1,0:T(8,128)(2,1)} %param.10) | copy-start | bytes 2359300
  6.5 46.9 %all-gather.18.cloned.1.call-start = ((), (), s32[]{:S(2)}) async-start(), calls=%async_computation.3 | async-start | bytes 3932160 | tf_op jit(solution)/shard_map/all_gather | solution.py:55
  7.3 70.8 %reduce-scatter.2.cloned.1.call-start = ((), (), s32[]{:S(2)}) async-start(), calls=%async_computation.1 | async-start | bytes 163840 | tf_op jit(solution)/shard_map/reduce_scatter | solution.py:47
  20.5 0.6 copy-start.4
  22.2 122.6 %all-reduce.2.cloned.1.call-start = ((), (), s32[]{:S(2)}) async-start(), calls=%async_computation.2 | async-start | bytes 4194304 | tf_op jit(solution)/shard_map/psum | solution.py:60
  56.7 0.9 copy-start.6
  57.6 2.7 copy-start.18
  60.2 93.6 %copy-start.17 = (s32[1,6]{1,0:T(1,128)S(1)}, s32[1,6]{1,0:T(1,128)}, u32[]{:S(2)}) copy-start(s32[1,6]{1,0:T(1,128)} %param.13) | copy-start | bytes 76
  60.2 93.7 %copy-start.16 = (f32[1,6,2,512]{3,2,1,0:T(2,128)S(1)}, f32[1,6,2,512]{3,2,1,0:T(2,128)}, u32[]{:S(2)}) copy-start(f32[1,6,2,512]{3,2,1,0:T(2,128)} %param.12) | copy-start | bytes 73732
  60.2 165.5 %all-gather.20.cloned.1.call-start = ((), (), s32[]{:S(2)}) async-start(), calls=%async_computation.4 | async-start | bytes 2129920 | tf_op jit(solution)/shard_map/all_gather | solution.py:74
  147.4 158.9 %all-gather.22.cloned.1.call-start = ((), (), s32[]{:S(2)}) async-start(), calls=%async_computation.5 | async-start | bytes 2129920 | tf_op jit(solution)/shard_map/all_gather | solution.py:74
  228.6 1.6 copy-start.2
  228.7 1.6 copy-start.3
  231.3 155.0 %all-gather.24.cloned.1.call-start = ((), (), s32[]{:S(2)}) async-start(), calls=%async_computation.6 | async-start | bytes 2129920 | tf_op jit(solution)/shard_map/all_gather | solution.py:74
  306.3 2.1 copy-start.11
  306.3 2.1 copy-start.12
  309.5 0.6 copy-start.9
  311.2 155.0 %all-gather.26.cloned.1.call-start = ((), (), s32[]{:S(2)}) async-start(), calls=%async_computation.7 | async-start | bytes 2129920 | tf_op jit(solution)/shard_map/all_gather | solution.py:74
  386.3 2.1 copy-start.13
  386.3 2.1 copy-start.14
  389.2 0.8 copy-start.10
  391.1 154.3 %all-gather.28.cloned.1.call-start = ((), (), s32[]{:S(2)}) async-start(), calls=%async_computation.8 | async-start | bytes 2129920 | tf_op jit(solution)/shard_map/all_gather | solution.py:74
  466.2 2.1 copy-start.15
  470.4 154.3 %all-gather.30.cloned.1.call-start = ((), (), s32[]{:S(2)}) async-start(), calls=%async_computation.9 | async-start | bytes 2129920 | tf_op jit(solution)/shard_map/all_gather | solution.py:74
  549.6 154.3 %all-gather.32.cloned.1.call-start = ((), (), s32[]{:S(2)}) async-start(), calls=%async_computation.10 | async-start | bytes 2129920 | tf_op jit(solution)/shard_map/all_gather | solution.py:74
  706.8 13.6 %copy-start.1 = (bf16[1,384,1536]{2,1,0:T(8,128)(2,1)S(1)}, bf16[1,384,1536]{2,1,0:T(8,128)(2,1)}, u32[]{:S(2)}) copy-start(bf16[1,384,1536]{2,1,0:T(8,128)(2,1)} %param.9) | copy-start | bytes 3538948
  706.8 12.6 %copy-start.5 = (f32[384,64]{0,1:T(8,128)S(1)}, f32[384,64]{0,1:T(8,128)}, u32[]{:S(2)}) copy-start(f32[384,64]{0,1:T(8,128)} %copy-done.4) | copy-start | bytes 294916
  706.8 12.6 %copy-start.7 = (bf16[384,1024]{1,0:T(8,128)(2,1)S(1)}, bf16[384,1024]{1,0:T(8,128)(2,1)}, u32[]{:S(2)}) copy-start(bf16[384,1024]{1,0:T(8,128)(2,1)} %copy-done.6) | copy-start | bytes 2359300
Sparse Core Ops, SparseCore 0:
  9.2 44.1 all-gather.17
  55.9 22.0 reduce-scatter.1
  80.5 64.2 all-reduce.1
  147.6 78.1 all-gather.19
  231.4 74.9 all-gather.21
  311.3 74.9 all-gather.23
  391.2 74.9 all-gather.25
  470.5 74.9 all-gather.27
  549.7 74.9 all-gather.29
  628.9 74.9 all-gather.31
where the time goes:
time: 728 us; the launch traced here: 727 us
  waiting for transfers between devices  629 us (86%)
  blocking collectives  25 us (3%)
  between operations  24.3 us (3%)
  other arithmetic  23.9 us (3%)
  matrix products  17 us (2%)
  local copies, waits for them, and re-layouts  7.96 us (1%)
    all_gather x7, waiting for transfers between devices, local(): make_piece = lax.all_gather(pattern[None], 'dom', axis=0, tiled=True)  513 us
    psum x1, waiting for transfers between devices, local(): coupling = lax.psum(partial_map.astype(jnp.bfloat16), 'sub')  66.8 us
    all_gather x1, waiting for transfers between devices, local(): lax.all_gather(disagg_rows, 'sub', axis=0, tiled=True)  31.2 us
    reduce_scatter x1, waiting for transfers between devices, local(): lax.psum_scatter(lax.dot_general(solved_half, agg_columns, CONTRACT_FIRST...  16.3 us
    convert_element_type x7, other arithmetic, rotate(): values = pattern.astype(jnp.float32)  14.6 us
  transfers between devices with their start and end apart: 10, of which 10 were waited for; matrix products, arithmetic and copies ran while one was open for 2% of the time, Pallas kernels for 0%

commit v1 on v0

--- a/solution.py
+++ b/solution.py
@@ -57,7 +57,9 @@
     partial_map = lax.dot_general(
         spread_half, agg_columns, CONTRACT_FIRST, preferred_element_type=jnp.float32
     )
-    coupling = lax.psum(partial_map.astype(jnp.bfloat16), "sub")
+    own = partial_map.astype(jnp.bfloat16)
+    parts = lax.all_gather(own, "sub", axis=0, tiled=False)
+    coupling = parts.sum(axis=0)
     domains = sweep_order.shape[0]
     segment_of = sweep_order * SEGMENTS // domains
     own_index = lax.axis_index("dom")

time: 728 us -> 755 us (1.037)
  waiting for transfers between devices: 629 us -> 652 us
    all_gather x0 -> x1, waiting for transfers between devices: none -> 72.6 us  [local(): parts = lax.all_gather(own, 'sub', axis=0, tiled=False)]
    psum x1 -> x0, waiting for transfers between devices: 66.8 us -> none  [local(): coupling = lax.psum(partial_map.astype(jnp.bfloat16), 'sub')]
    all_gather x1, waiting for transfers between devices: 31.2 us -> 46.1 us  [local(): lax.all_gather(disagg_rows, 'sub', axis=0, tiled=True)]
where the time goes in v1:
time: 755 us; the launch traced here: 754 us
  waiting for transfers between devices  652 us (86%)
  other arithmetic  30.5 us (4%)
  between operations  24.3 us (3%)
  blocking collectives  23.5 us (3%)
  matrix products  16.3 us (2%)
    all_gather x7, waiting for transfers between devices, local(): make_piece = lax.all_gather(pattern[None], 'dom', axis=0, tiled=True)  514 us
    all_gather x1, waiting for transfers between devices, local(): parts = lax.all_gather(own, 'sub', axis=0, tiled=False)  72.6 us
    all_gather x1, waiting for transfers between devices, local(): lax.all_gather(disagg_rows, 'sub', axis=0, tiled=True)  46.1 us
    reduce_scatter x1, waiting for transfers between devices, local(): lax.psum_scatter(lax.dot_general(solved_half, agg_columns, CONTRACT_FIRST...  18.1 us
  transfers between devices with their start and end apart: 10, of which 10 were waited for; matrix products, arithmetic and copies ran while one was open for 2% of the time, Pallas kernels for 0%

profile of v1, /device:TPU:8, one launch (start us, length us, event | category | flops | bytes accessed | tf_op | source)
XLA Modules:
  0.0 754.2 jit_solution(1682828596675708405)
XLA Ops:
  6.5 0.7 all-gather.20.cloned.1.call-update
  7.3 46.1 %all-gather.20.cloned.1.call-done = bf16[1,1536,1024]{2,1,0:T(8,128)(2,1)} async-done(((bf16[1,384,1024]{2,1,0:T(8,128)(2,1)}), bf16[1,1536,1024]{2,1,0:T(8,128)(2,1)}) %all-gather.20.cloned.1.call-update) | async-done | bytes 3145744 | tf_op jit(solution)/shard_map/all_gather | solution.py:55
  53.4 3.3 fusion.2
  56.7 2.7 convolution_convert_fusion
  59.4 0.0 reduce-scatter.2.cloned.1.call-start
  59.5 11.2 %all-gather = bf16[1,1536,64]{1,2,0:T(8,128)(2,1)S(1)} all-gather(bf16[1,384,64]{1,2,0:T(8,128)(2,1)S(1)} %copy-done.17), channel_id=2, replica_groups=mesh['dom'=64,'sub'=4] {'sub'}, dimensions={1}, use_global_device_ids=true | all-gather | bytes 245760 | tf_op jit(solution)/shard_map/all_gather | solution.py:45
  70.7 0.5 fusion.6
  71.2 1.0 convolution_convert_fusion.1
  72.2 0.0 all-gather.24.cloned.1.call-start
  72.3 0.7 dynamic_slice.3
  73.7 72.6 %all-gather.22.cloned.1.call-done = bf16[4096,1024]{1,0:T(8,128)(2,1)} async-done(((bf16[1024,1024]{1,0:T(8,128)(2,1)}), bf16[4096,1024]{1,0:T(8,128)(2,1)}) %all-gather.22.cloned.1.call-update) | async-done | bytes 8388624 | tf_op jit(solution)/shard_map/all_gather | solution.py:61
  146.3 6.5 reduce_sum.148
  152.8 18.1 %reduce-scatter.2.cloned.1.call-done = bf16[16,1024]{1,0:T(8,128)(2,1)} async-done(((bf16[64,1024]{1,0:T(8,128)(2,1)}), bf16[16,1024]{1,0:T(8,128)(2,1)}) %reduce-scatter.2.cloned.1.call-update) | async-done | bytes 32784 | tf_op jit(solution)/shard_map/reduce_scatter | solution.py:47
  170.9 1.8 fusion.10
  172.7 0.0 all-gather.26.cloned.1.call-start
  178.9 0.1 select_reduce_fusion.7
  179.1 0.1 fusion.42
  179.2 1.9 select_reduce_fusion
  181.0 0.7 slice_bitcast_fusion.13
  181.8 70.9 %all-gather.24.cloned.1.call-done = bf16[1024,1024]{1,0:T(8,128)(2,1)} async-done(((bf16[16,1024]{1,0:T(8,128)(2,1)}), bf16[1024,1024]{1,0:T(8,128)(2,1)}) %all-gather.24.cloned.1.call-update) | async-done | bytes 2097168 | tf_op jit(solution)/shard_map/all_gather | solution.py:76
  252.7 2.1 convert.1
  254.8 0.8 multiply_subtract_fusion.6
  255.7 0.2 maximum_reduce_fusion
  255.9 0.6 copy-done.6
  256.5 1.0 fusion.22
  257.6 0.0 all-gather.28.cloned.1.call-start
  258.3 1.7 slice_bitcast_fusion.11
  260.0 72.6 %all-gather.26.cloned.1.call-done = bf16[1024,1024]{1,0:T(8,128)(2,1)} async-done(((bf16[16,1024]{1,0:T(8,128)(2,1)}), bf16[1024,1024]{1,0:T(8,128)(2,1)}) %all-gather.26.cloned.1.call-update) | async-done | bytes 2097168 | tf_op jit(solution)/shard_map/all_gather | solution.py:76
  332.6 2.1 convert.2
  334.8 0.8 multiply_subtract_fusion.5
  335.6 0.2 maximum_reduce_fusion.1
  335.8 0.6 copy-done.7
  336.5 0.6 copy-done.8
  337.1 1.0 fusion.21
  338.1 0.2 all-gather.30.cloned.1.call-start
  339.0 0.7 slice_bitcast_fusion.9
  339.8 73.4 %all-gather.28.cloned.1.call-done = bf16[1024,1024]{1,0:T(8,128)(2,1)} async-done(((bf16[16,1024]{1,0:T(8,128)(2,1)}), bf16[1024,1024]{1,0:T(8,128)(2,1)}) %all-gather.28.cloned.1.call-update) | async-done | bytes 2097168 | tf_op jit(solution)/shard_map/all_gather | solution.py:76
  413.2 2.1 convert.3
  415.3 0.8 multiply_subtract_fusion.4
  416.1 0.2 maximum_reduce_fusion.2
  416.4 0.6 copy-done.9
  417.0 1.0 fusion.20
  418.8 0.7 slice_bitcast_fusion.7
  419.4 73.7 %all-gather.30.cloned.1.call-done = bf16[1024,1024]{1,0:T(8,128)(2,1)} async-done(((bf16[16,1024]{1,0:T(8,128)(2,1)}), bf16[1024,1024]{1,0:T(8,128)(2,1)}) %all-gather.30.cloned.1.call-update) | async-done | bytes 2097168 | tf_op jit(solution)/shard_map/all_gather | solution.py:76
  493.1 2.1 convert.4
  495.2 0.8 multiply_subtract_fusion.3
  496.0 0.2 maximum_reduce_fusion.3
  496.3 1.0 fusion.19
  498.1 74.3 %all-gather.32.cloned.1.call-done = bf16[1024,1024]{1,0:T(8,128)(2,1)} async-done(((bf16[16,1024]{1,0:T(8,128)(2,1)}), bf16[1024,1024]{1,0:T(8,128)(2,1)}) %all-gather.32.cloned.1.call-update) | async-done | bytes 2097168 | tf_op jit(solution)/shard_map/all_gather | solution.py:76
  572.4 2.1 convert.5
  574.5 0.8 multiply_subtract_fusion.2
  575.3 0.2 maximum_reduce_fusion.4
  575.5 1.0 fusion.18
  577.3 74.3 %all-gather.34.cloned.1.call-done = bf16[1024,1024]{1,0:T(8,128)(2,1)} async-done(((bf16[16,1024]{1,0:T(8,128)(2,1)}), bf16[1024,1024]{1,0:T(8,128)(2,1)}) %all-gather.34.cloned.1.call-update) | async-done | bytes 2097168 | tf_op jit(solution)/shard_map/all_gather | solution.py:76
  651.6 2.1 convert.6
  653.7 0.8 multiply_subtract_fusion.1
  654.5 0.2 maximum_reduce_fusion.5
  654.7 1.0 fusion.17
  655.8 75.0 %all-gather.36.cloned.1.call-done = bf16[1024,1024]{1,0:T(8,128)(2,1)} async-done(((bf16[16,1024]{1,0:T(8,128)(2,1)}), bf16[1024,1024]{1,0:T(8,128)(2,1)}) %all-gather.36.cloned.1.call-update) | async-done | bytes 2097168 | tf_op jit(solution)/shard_map/all_gather | solution.py:76
  730.9 2.1 convert.7
  732.9 0.8 multiply_subtract_fusion
  733.8 0.2 maximum_reduce_fusion.6
  734.0 12.3 %all_gather.47 = bf16[64,1024]{1,0:T(8,128)(2,1)S(1)} all-gather(bf16[16,1024]{1,0:T(8,128)(2,1)S(1)} %add_convert_fusion), channel_id=1, replica_groups=mesh['dom'=64,'sub'=4] {'sub'}, dimensions={0}, use_global_device_ids=true | all-gather | bytes 163840 | tf_op jit(solution)/shard_map/all_gather | solution.py:94
  746.3 1.0 fusion.8
  (64 shorter events, 0.5 us)
Async XLA Ops:
  6.5 46.9 %copy-start = (bf16[1,384,1536]{2,1,0:T(8,128)(2,1)S(1)}, bf16[1,384,1536]{2,1,0:T(8,128)(2,1)}, u32[]{:S(2)}) copy-start(bf16[1,384,1536]{2,1,0:T(8,128)(2,1)} %param.9) | copy-start | bytes 3538948
  6.5 46.9 %all-gather.20.cloned.1.call-start = ((), (), s32[]{:S(2)}) async-start(), calls=%async_computation.2 | async-start | bytes 3932160 | tf_op jit(solution)/shard_map/all_gather | solution.py:55
  7.3 49.4 %copy-start.5 = (bf16[1,1024,384]{2,1,0:T(8,128)(2,1)S(1)}, bf16[1,1024,384]{2,1,0:T(8,128)(2,1)}, u32[]{:S(2)}) copy-start(bf16[1,1024,384]{2,1,0:T(8,128)(2,1)} %param.10) | copy-start | bytes 2359300
  7.3 139.0 %all-gather.22.cloned.1.call-start = ((), (), s32[]{:S(2)}) async-start(), calls=%async_computation.3 | async-start | bytes 10485760 | tf_op jit(solution)/shard_map/all_gather | solution.py:61
  56.7 2.7 copy-start.3
  56.7 2.8 copy-start.17
  59.4 12.9 %copy-start.20 = (s32[64]{0:T(128)S(1)}, s32[64]{0:T(128)}, u32[]{:S(2)}) copy-start(s32[64]{0:T(128)} %param.15) | copy-start | bytes 772
  59.4 111.5 %reduce-scatter.2.cloned.1.call-start = ((), (), s32[]{:S(2)}) async-start(), calls=%async_computation.1 | async-start | bytes 163840 | tf_op jit(solution)/shard_map/reduce_scatter | solution.py:47
  72.2 180.5 %all-gather.24.cloned.1.call-start = ((), (), s32[]{:S(2)}) async-start(), calls=%async_computation.4 | async-start | bytes 2129920 | tf_op jit(solution)/shard_map/all_gather | solution.py:76
  152.8 26.3 %copy-start.19 = (s32[1,6]{1,0:T(1,128)S(1)}, s32[1,6]{1,0:T(1,128)}, u32[]{:S(2)}) copy-start(s32[1,6]{1,0:T(1,128)} %param.13) | copy-start | bytes 76
  152.8 26.4 %copy-start.18 = (f32[1,6,2,512]{3,2,1,0:T(2,128)S(1)}, f32[1,6,2,512]{3,2,1,0:T(2,128)}, u32[]{:S(2)}) copy-start(f32[1,6,2,512]{3,2,1,0:T(2,128)} %param.12) | copy-start | bytes 73732
  172.7 159.9 %all-gather.26.cloned.1.call-start = ((), (), s32[]{:S(2)}) async-start(), calls=%async_computation.5 | async-start | bytes 2129920 | tf_op jit(solution)/shard_map/all_gather | solution.py:76
  252.7 2.1 copy-start.10
  252.7 2.1 copy-start.11
  255.7 0.9 copy-start.2
  255.9 0.6 copy-start.6
  257.6 155.6 %all-gather.28.cloned.1.call-start = ((), (), s32[]{:S(2)}) async-start(), calls=%async_computation.6 | async-start | bytes 2129920 | tf_op jit(solution)/shard_map/all_gather | solution.py:76
  332.6 2.1 copy-start.12
  332.6 2.1 copy-start.13
  335.6 0.8 copy-start.7
  336.5 0.6 copy-start.8
  338.1 155.0 %all-gather.30.cloned.1.call-start = ((), (), s32[]{:S(2)}) async-start(), calls=%async_computation.7 | async-start | bytes 2129920 | tf_op jit(solution)/shard_map/all_gather | solution.py:76
  413.2 2.1 copy-start.14
  413.2 2.1 copy-start.15
  416.1 0.8 copy-start.9
  418.0 154.4 %all-gather.32.cloned.1.call-start = ((), (), s32[]{:S(2)}) async-start(), calls=%async_computation.8 | async-start | bytes 2129920 | tf_op jit(solution)/shard_map/all_gather | solution.py:76
  493.1 2.1 copy-start.16
  497.3 154.3 %all-gather.34.cloned.1.call-start = ((), (), s32[]{:S(2)}) async-start(), calls=%async_computation.9 | async-start | bytes 2129920 | tf_op jit(solution)/shard_map/all_gather | solution.py:76
  576.5 154.3 %all-gather.36.cloned.1.call-start = ((), (), s32[]{:S(2)}) async-start(), calls=%async_computation.10 | async-start | bytes 2129920 | tf_op jit(solution)/shard_map/all_gather | solution.py:76
  733.7 13.6 %copy-start.1 = (bf16[1,384,1536]{2,1,0:T(8,128)(2,1)S(1)}, bf16[1,384,1536]{2,1,0:T(8,128)(2,1)}, u32[]{:S(2)}) copy-start(bf16[1,384,1536]{2,1,0:T(8,128)(2,1)} %param.9) | copy-start | bytes 3538948
  733.7 12.6 %copy-start.4 = (bf16[384,1024]{1,0:T(8,128)(2,1)S(1)}, bf16[384,1024]{1,0:T(8,128)(2,1)}, u32[]{:S(2)}) copy-start(bf16[384,1024]{1,0:T(8,128)(2,1)} %copy-done.3) | copy-start | bytes 2359300
Sparse Core Ops, SparseCore 0:
  9.2 44.1 all-gather.19
  59.5 86.6 all-gather.21
  148.8 22.0 reduce-scatter.1
  173.9 78.7 all-gather.23
  257.7 74.9 all-gather.25
  338.2 74.9 all-gather.27
  418.1 74.9 all-gather.29
  497.4 74.9 all-gather.31
  576.7 74.9 all-gather.33
  655.9 74.9 all-gather.35
